TPU v7x, 512 devices: a whole 4x4x16 slice. The times are simulated.
512 devices in a mesh: expert: 64 (over x_hi, z, core), dp: 8 (over x_lo, y).
Axes of the slice: x: 4 (x_hi: 2, x_lo: 2; x = x_hi * 2 + x_lo), y: 4, z: 16, core: 2. Of those that a mesh axis runs over, the one named last changes fastest.
Arguments:
- skip_stream: bfloat16 [4096, 4096], P(('expert', 'dp')), may hold values from -6 to 6
- attention_probes: bfloat16 [4096, 4096], P(('expert', 'dp')), may hold values from -5 to 5
- stored_attention_lookups: bfloat16 [4096, 16, 512], P(('expert', 'dp')), may hold values from -5 to 5
- stored_attention_contents: bfloat16 [4096, 16, 512], P(('expert', 'dp')), may hold values from -6 to 6
- incoming_lookup_entries: bfloat16 [4096, 512], P(('expert', 'dp')), may hold values from -6 to 6
- incoming_content_entries: bfloat16 [4096, 512], P(('expert', 'dp')), may hold values from -6 to 6
- filled_slot_spans: int32 [4096], P(('expert', 'dp')), may hold values from 2 to 16, as said below
- layernorm_gain: float32 [4096], replicated, may hold values from 0.1 to 1.9
- routed_specialist_indices: int32 [4096, 8], P(('expert', 'dp')), may hold values from 0 to 63, all different within a row; in each aligned block of 8 rows (0 to 7, 8 to 15, ...) at most 2 rows name the same one
- routing_probabilities: float32 [4096, 8], P(('expert', 'dp')), may hold values from 0.05 to 1
- admission_limits: int32 [64], replicated, may hold values from 256 to 1024
- swap_indicator: int32 [64], replicated, may hold values from 0 to 1, as said below
- gating_projection_matrix: bfloat16 [64, 768, 4096], P('expert', 'dp'), may hold values from -0.09375 to 0.09375
- widening_projection_matrix: bfloat16 [64, 768, 4096], P('expert', 'dp'), may hold values from -0.09375 to 0.09375
- output_projection_matrix: bfloat16 [64, 768, 4096], P('expert', None, 'dp'), may hold values from -0.21875 to 0.21875
Outputs:
- layer_out: bfloat16 [4096, 4096], P(('expert', 'dp'))
- device_share: float32 [64], P('expert')
- held_gate: bfloat16 [64, 768, 4096], P('expert', 'dp')
- held_up: bfloat16 [64, 768, 4096], P('expert', 'dp')
- held_down: bfloat16 [64, 768, 4096], P('expert', None, 'dp')
Inputs may be any that keep to these rules, and one draw needn't show every extreme that they name: `filled_slot_spans`: each sequence has 2 or more valid slots and some sequence has all 16. `routed_specialist_indices`: in each aligned block of 8 rows (the rows of one device) no expert is named by more than 2 rows; the entries of a row differ. swap_indicator[i] equals swap_indicator[i + 32].
All inputs are finite; a program needn't handle non-finite values.
Results may differ from a plain program's by a relative error of at most 0.017.
Values may be sent and summed in bfloat16 or wider, within the bound.
No kernel may reach another device: no remote copies, remote signals or barrier semaphores. Data moves between devices by JAX's collectives and lax.ppermute only.
A program may use at most 64 MiB of HBM per device.

v0:
```python
import jax
import jax.numpy as jnp
from jax import lax
from jax.sharding import PartitionSpec as P

QH = 32
KVH = 4
HEAD = 128


def swapped(value, axis, stride):
    mask = 2**stride
    pairs = [(source, source ^ mask) for source in range(lax.axis_size(axis))]
    return lax.ppermute(value, axis, pairs)


def attention(query_rows, key_rows, value_rows, new_key, new_value, valid_len):
    seq_count = query_rows.shape[0]
    cache_len = key_rows.shape[1]
    group = QH // KVH
    scale = HEAD ** (-0.5)
    query_view = query_rows.reshape(seq_count, KVH, group, HEAD)
    key_view = key_rows.reshape(seq_count, cache_len, KVH, HEAD)
    value_view = value_rows.reshape(seq_count, cache_len, KVH, HEAD)
    scores = (
        jnp.einsum("skgd,slkd->skgl", query_view, key_view, preferred_element_type=jnp.float32)
        * scale
    )
    valid = lax.broadcasted_iota(jnp.int32, (seq_count, cache_len), 1) < valid_len[:, None]
    scores = jnp.where(valid[:, None, None, :], scores, -1e30)
    own_score = (
        jnp.einsum(
            "skgd,skd->skg",
            query_view,
            new_key.reshape(seq_count, KVH, HEAD),
            preferred_element_type=jnp.float32,
        )
        * scale
    )
    highest = jnp.maximum(jnp.max(scores, axis=-1), own_score)
    weights = jnp.exp(scores - highest[..., None])
    own_weight = jnp.exp(own_score - highest)
    denom = jnp.sum(weights, axis=-1) + own_weight
    probs = (weights / denom[..., None]).astype(jnp.bfloat16)
    own_prob = (own_weight / denom).astype(jnp.bfloat16)
    mixed = jnp.einsum("skgl,slkd->skgd", probs, value_view, preferred_element_type=jnp.float32)
    mixed = mixed + own_prob.astype(jnp.float32)[..., None] * new_value.reshape(
        seq_count, KVH, 1, HEAD
    ).astype(jnp.float32)
    return mixed.reshape(seq_count, QH * HEAD).astype(jnp.bfloat16)


def per_device(
    skip_stream,
    attention_probes,
    stored_attention_lookups,
    stored_attention_contents,
    incoming_lookup_entries,
    incoming_content_entries,
    filled_slot_spans,
    layernorm_gain,
    routed_specialist_indices,
    routing_probabilities,
    admission_limits,
    swap_indicator,
    gating_projection_matrix,
    widening_projection_matrix,
    output_projection_matrix,
):
    experts = lax.axis_size("expert")
    groups = lax.axis_size("dp")
    half_axis = experts // 2
    far_bit = experts.bit_length() - 2
    my_index = lax.axis_index("expert")
    my_device = my_index * groups + lax.axis_index("dp")
    own_weights = (
        gating_projection_matrix[0],
        widening_projection_matrix[0],
        output_projection_matrix[0],
    )
    partner = swapped(own_weights, "expert", far_bit)
    take_other = swap_indicator[my_index] == 1
    gate_held = jnp.where(take_other, partner[0], own_weights[0])
    up_held = jnp.where(take_other, partner[1], own_weights[1])
    down_held = jnp.where(take_other, partner[2], own_weights[2])
    retained_specialist = jnp.where(take_other, (my_index + half_axis) % experts, my_index)
    seq_rows = skip_stream.shape[0]
    top_count = routed_specialist_indices.shape[1]
    width = skip_stream.shape[1]
    slot_cap = 2
    expert_range = lax.broadcasted_iota(jnp.int32, (experts,), 0)
    all_routes = lax.all_gather(routed_specialist_indices, ("expert", "dp"), axis=0, tiled=True)
    all_hot = jnp.sum(
        (all_routes[:, :, None] == expert_range[None, None, :]).astype(jnp.int32), axis=1
    )
    all_rows = lax.broadcasted_iota(jnp.int32, (all_routes.shape[0], 1), 0)
    before_mine = jnp.sum(jnp.where(all_rows < my_device * seq_rows, all_hot, 0), axis=0)
    tallies = jnp.sum(all_hot, axis=0)
    route_hot = (routed_specialist_indices[:, :, None] == expert_range[None, None, :]).astype(
        jnp.int32
    )
    row_hot = jnp.sum(route_hot, axis=1)
    earlier = jnp.cumsum(row_hot, axis=0) - row_hot
    local_rank = jnp.sum(route_hot * earlier[:, None, :], axis=-1)
    global_rank = local_rank + jnp.sum(route_hot * before_mine[None, None, :], axis=-1)
    pair_limit = jnp.sum(route_hot * admission_limits[None, None, :], axis=-1)
    kept = global_rank < pair_limit
    held_tally = jnp.sum(jnp.where(expert_range == retained_specialist, tallies, 0))
    device_share = jnp.minimum(held_tally, admission_limits[retained_specialist]).astype(
        jnp.float32
    ) / (seq_rows * top_count * groups)
    attn = attention(
        attention_probes,
        stored_attention_lookups,
        stored_attention_contents,
        incoming_lookup_entries,
        incoming_content_entries,
        filled_slot_spans,
    )
    stream = skip_stream.astype(jnp.float32) + attn.astype(jnp.float32)
    normed = (
        stream
        * lax.rsqrt(jnp.mean(stream * stream, axis=-1, keepdims=True) + 1e-06)
        * layernorm_gain
    ).astype(jnp.bfloat16)
    slot_code = routed_specialist_indices * slot_cap + local_rank
    targets = lax.broadcasted_iota(jnp.int32, (experts * slot_cap,), 0)
    slot_hits = jnp.any(slot_code[:, :, None] == targets[None, None, :], axis=1)
    occupied = jnp.any(slot_hits, axis=0)
    row_range = lax.broadcasted_iota(jnp.int32, (seq_rows, 1), 0)
    source_row = jnp.sum(jnp.where(slot_hits, row_range, 0), axis=0) + jnp.where(
        occupied, 0, seq_rows
    )
    padded_rows = jnp.concatenate([normed, jnp.zeros((1, width), jnp.bfloat16)], axis=0)
    outgoing = padded_rows[source_row].reshape(experts, slot_cap, width)
    arrived_rows = lax.all_to_all(outgoing, "expert", split_axis=0, concat_axis=0, tiled=True)
    column_rows = lax.all_gather(arrived_rows, "dp", axis=1, tiled=True)
    gate_val = jnp.einsum(
        "esf,hf->esh", column_rows, own_weights[0], preferred_element_type=jnp.float32
    )
    up_val = jnp.einsum(
        "esf,hf->esh", column_rows, own_weights[1], preferred_element_type=jnp.float32
    )
    hidden = (jax.nn.silu(gate_val) * up_val).astype(jnp.bfloat16)
    feature_cols = own_weights[2].shape[1]
    summed = jnp.einsum(
        "esn,nf->esf",
        lax.all_gather(hidden, "dp", axis=2, tiled=True),
        own_weights[2],
        preferred_element_type=jnp.float32,
    )
    results = summed.astype(jnp.bfloat16).reshape(experts, groups, slot_cap, feature_cols)
    returned = lax.all_to_all(
        lax.all_to_all(results, "expert", split_axis=0, concat_axis=0, tiled=True),
        "dp",
        split_axis=1,
        concat_axis=3,
        tiled=True,
    )
    returned_flat = returned.reshape(experts * slot_cap, width)
    picked = returned_flat[slot_code]
    factor = jnp.where(kept, routing_probabilities, 0.0)
    expert_mix = jnp.sum(factor[:, :, None] * picked.astype(jnp.float32), axis=1)
    layer_out = (stream + expert_mix).astype(jnp.bfloat16)
    return (layer_out, device_share.reshape(1), gate_held[None], up_held[None], down_held[None])


def solution(mesh):
    in_specs = (
        P(("expert", "dp"), None),
        P(("expert", "dp"), None),
        P(("expert", "dp"), None, None),
        P(("expert", "dp"), None, None),
        P(("expert", "dp"), None),
        P(("expert", "dp"), None),
        P(("expert", "dp")),
        P(),
        P(("expert", "dp"), None),
        P(("expert", "dp"), None),
        P(),
        P(),
        P("expert", "dp", None),
        P("expert", "dp", None),
        P("expert", None, "dp"),
    )
    out_specs = (
        P(("expert", "dp"), None),
        P("expert"),
        P("expert", "dp", None),
        P("expert", "dp", None),
        P("expert", None, "dp"),
    )
    return jax.shard_map(
        per_device, mesh=mesh, in_specs=in_specs, out_specs=out_specs, check_vma=False
    )
```

profile of v0, /device:TPU:1, one launch (start us, length us, event | category | flops | bytes accessed | tf_op | source)
XLA Modules:
  0.0 1606.2 jit_solution(4724986277860716594)
XLA Ops:
  7.3 1247.2 %all_gather.9 = s32[4096,8]{1,0:T(8,128)S(1)} all-gather(s32[8,8]{1,0:T(8,128)} %param.23), channel_id=1, replica_groups=mesh['expert'=64,'dp'=8] {'expert','dp'}, dimensions={0}, use_global_device_ids=true | all-gather | bytes 131328 | tf_op jit(solution)/shard_map/all_gather | solution.py:92
  1261.1 1.9 convert_reduce_fusion
  1266.0 72.0 %all_to_all.25 = bf16[64,2,4096]{2,1,0:T(2,128)(2,1)S(1)} all-to-all(bf16[64,2,4096]{2,1,0:T(2,128)(2,1)S(1)} %reshape.129), channel_id=1, replica_groups=mesh['expert'=64,'dp'=8] {'expert'}, dimensions={0} | all-to-all | bytes 2097152 | tf_op jit(solution)/shard_map/all_to_all | solution.py:136
  1338.0 1.7 copy.49
  1339.9 92.2 %all-gather.3.cloned.1.call-done = bf16[64,16,4096]{2,0,1:T(8,128)(2,1)} async-done(((bf16[64,2,4096]{2,0,1:T(8,128)(2,1)}), bf16[64,16,4096]{2,0,1:T(8,128)(2,1)}) %all-gather.3.cloned.1.call-update) | async-done | bytes 8388624 | tf_op jit(solution)/shard_map/all_gather | solution.py:137
  1432.1 5.8 fusion.8
  1438.0 2.4 fusion
  1441.5 48.3 %all-gather.5.cloned.1.call-done = bf16[64,16,768]{0,1,2:T(8,128)(2,1)} async-done(((bf16[64,16,96]{0,1,2:T(8,128)(2,1)}), bf16[64,16,768]{0,1,2:T(8,128)(2,1)}) %all-gather.5.cloned.1.call-update) | async-done | bytes 1572880 | tf_op jit(solution)/shard_map/all_gather | solution.py:148
  1489.8 5.5 copy.51
  1495.3 2.1 convolution_convert_fusion
  1497.4 1.2 reshape.130
  1498.7 18.1 %all-to-all-start.1 = ((bf16[64,8,2,512]{3,2,1,0:T(2,128)(2,1)}), bf16[64,8,2,512]{3,2,1,0:T(2,128)(2,1)S(1)}, u32[]{:S(2)}, u32[]{:S(2)}) async-start(bf16[64,8,2,512]{3,2,1,0:T(2,128)(2,1)} %reshape.130), calls=%async_computation.1 | async-start | bytes 2097152 | tf_op jit(solution)/shard_map/all_to_all | solution.py:154
  1516.7 4.9 collective-permute-start.2
  1521.7 1.9 collective-permute-start.1
  1523.6 4.9 collective-permute-start
  1532.4 10.7 collective-permute-done.2
  1543.1 2.1 select_bitcast_fusion
  1545.2 20.9 %collective-permute-done.1 = bf16[96,4096]{1,0:T(8,128)(2,1)S(1)} collective-permute-done((bf16[96,4096]{1,0:T(8,128)(2,1)}, bf16[96,4096]{1,0:T(8,128)(2,1)S(1)}, u32[]{:S(2)}, u32[]{:S(2)}) %collective-permute-start.1) | collective-permute-done | bytes 786464 | tf_op jit(solution)/shard_map/ppermute | solution.py:14
  1566.1 2.1 select_bitcast_fusion.1
  1568.6 1.8 copy.52
  1570.4 3.8 all-to-all-start.2
  1574.2 9.1 collective-permute-done
  1583.3 2.1 select_bitcast_fusion.2
  1585.4 9.3 all-to-all-done.2
  (64 shorter events, 16.7 us)
Async XLA Ops:
  7.2 1252.0 %copy-start = (bf16[8,16,512]{2,1,0:T(8,128)(2,1)S(1)}, bf16[8,16,512]{2,1,0:T(8,128)(2,1)}, u32[]{:S(2)}) copy-start(bf16[8,16,512]{2,1,0:T(8,128)(2,1)} %param.18) | copy-start | bytes 393220
  7.2 1256.0 %copy-start.4 = (s32[8,8]{1,0:T(8,128)S(1)}, s32[8,8]{1,0:T(8,128)}, u32[]{:S(2)}) copy-start(s32[8,8]{1,0:T(8,128)} %param.23) | copy-start | bytes 772
  7.2 1256.7 %copy-start.3 = (bf16[8,4096]{1,0:T(8,128)(2,1)S(1)}, bf16[8,4096]{1,0:T(8,128)(2,1)}, u32[]{:S(2)}) copy-start(bf16[8,4096]{1,0:T(8,128)(2,1)} %param.15) | copy-start | bytes 196612
  7.2 1256.0 %copy-start.7 = (s32[64]{0:T(128)S(1)}, s32[64]{0:T(128)}, u32[]{:S(2)}) copy-start(s32[64]{0:T(128)} %param.25) | copy-start | bytes 772
  7.2 1256.7 %copy-start.5 = (f32[4096]{0:T(1024)S(1)}, f32[4096]{0:T(1024)}, u32[]{:S(2)}) copy-start(f32[4096]{0:T(1024)} %param.22) | copy-start | bytes 49156
  7.2 1424.9 %all-gather.3.cloned.1.call-start = ((), (), s32[]{:S(2)}) async-start(), calls=%async_computation.3 | async-start | bytes 9437184 | tf_op jit(solution)/shard_map/all_gather | solution.py:137
  1264.0 168.1 %copy-start.2 = (bf16[1,96,4096]{2,1,0:T(8,128)(2,1)S(1)}, bf16[1,96,4096]{2,1,0:T(8,128)(2,1)}, u32[]{:S(2)}) copy-start(bf16[1,96,4096]{2,1,0:T(8,128)(2,1)} %param.27) | copy-start | bytes 2359300
  1339.7 98.3 %copy-start.1 = (bf16[1,96,4096]{2,1,0:T(8,128)(2,1)S(1)}, bf16[1,96,4096]{2,1,0:T(8,128)(2,1)}, u32[]{:S(2)}) copy-start(bf16[1,96,4096]{2,1,0:T(8,128)(2,1)} %param.28) | copy-start | bytes 2359300
  1339.7 150.1 %all-gather.5.cloned.1.call-start = ((), (), s32[]{:S(2)}) async-start(), calls=%async_computation.4 | async-start | bytes 3538944 | tf_op jit(solution)/shard_map/all_gather | solution.py:148
  1432.1 5.9 copy-start.8
  1440.4 88.1 %copy-start.9 = (s32[64]{0:T(128)S(1)}, s32[64]{0:T(128)}, u32[]{:S(2)}) copy-start(s32[64]{0:T(128)} %param.26) | copy-start | bytes 772
  1440.4 91.9 %copy-start.6 = (f32[8,8]{1,0:T(8,128)S(1)}, f32[8,8]{1,0:T(8,128)}, u32[]{:S(2)}) copy-start(f32[8,8]{1,0:T(8,128)} %param.24) | copy-start | bytes 772
  1498.7 69.9 %all-to-all-start.1 = ((bf16[64,8,2,512]{3,2,1,0:T(2,128)(2,1)}), bf16[64,8,2,512]{3,2,1,0:T(2,128)(2,1)S(1)}, u32[]{:S(2)}, u32[]{:S(2)}) async-start(bf16[64,8,2,512]{3,2,1,0:T(2,128)(2,1)} %reshape.130), calls=%async_computation.1 | async-start | bytes 2097152 | tf_op jit(solution)/shard_map/all_to_all | solution.py:154
  1516.7 26.4 %collective-permute-start.2 = (bf16[768,512]{1,0:T(8,128)(2,1)}, bf16[768,512]{1,0:T(8,128)(2,1)}, u32[]{:S(2)}, u32[]{:S(2)}) collective-permute-start(bf16[768,512]{1,0:T(8,128)(2,1)} %bitcast.80), channel_id=1, source_target_pairs={{0,256},{8,264},{16,272},{24,280},{32,288},{40,296},{48,304},{56,3... | collective-permute-start | bytes 2359304 | tf_op jit(solution)/shard_map/ppermute | solution.py:14
  1521.7 44.5 %collective-permute-start.1 = (bf16[96,4096]{1,0:T(8,128)(2,1)}, bf16[96,4096]{1,0:T(8,128)(2,1)S(1)}, u32[]{:S(2)}, u32[]{:S(2)}) collective-permute-start(bf16[96,4096]{1,0:T(8,128)(2,1)} %bitcast.81), channel_id=1, source_target_pairs={{0,256},{8,264},{16,272},{24,280},{32,288},{40,296},{48,304},{56,3... | collective-permute-start | bytes 2359304 | tf_op jit(solution)/shard_map/ppermute | solution.py:14
  1523.6 59.7 %collective-permute-start = (bf16[96,4096]{1,0:T(8,128)(2,1)}, bf16[96,4096]{1,0:T(8,128)(2,1)S(1)}, u32[]{:S(2)}, u32[]{:S(2)}) collective-permute-start(bf16[96,4096]{1,0:T(8,128)(2,1)} %bitcast.82), channel_id=1, source_target_pairs={{0,256},{8,264},{16,272},{24,280},{32,288},{40,296},{48,304},{56,3... | collective-permute-start | bytes 2359304 | tf_op jit(solution)/shard_map/ppermute | solution.py:14
  1570.4 24.3 %all-to-all-start.2 = ((bf16[64,8,2,512]{3,2,0,1:T(2,128)(2,1)}), bf16[64,8,2,512]{3,2,0,1:T(2,128)(2,1)S(1)}, u32[]{:S(2)}, u32[]{:S(2)}) async-start(bf16[64,8,2,512]{3,2,0,1:T(2,128)(2,1)} %copy.52), calls=%async_computation.2 | async-start | bytes 2097152 | tf_op jit(solution)/shard_map/all_to_all | solution.py:153
Sparse Core Ops, SparseCore 0:
  1339.8 92.2 all-gather.2
  1441.6 48.1 all-gather.4
where the time goes:
time: 1610 us
  blocking collectives  1320 us (82%)
  waiting for transfers between devices  191 us (12%)
  starting transfers between devices  33.8 us (2%)
  between operations  17.5 us (1%)
  local copies, waits for them, and re-layouts  17.4 us (1%)
    all_gather x1, blocking collectives, per_device(): lax.all_gather(routed_specialist_indices, ('expert', 'dp'), axis=0, tiled...  1250 us
    all_gather x1, waiting for transfers between devices, per_device(): column_rows = lax.all_gather(arrived_rows, 'dp', axis=1, tiled=True)  92.2 us
    all_to_all x1, blocking collectives, per_device(): lax.all_to_all(outgoing, 'expert', split_axis=0, concat_axis=0, tiled=True)  72 us
    all_gather x1, waiting for transfers between devices, per_device(): lax.all_gather(hidden, 'dp', axis=2, tiled=True)  48.3 us
    ppermute x3, waiting for transfers between devices, swapped(): return lax.ppermute(value, axis, pairs)  40.8 us
  transfers between devices with their start and end apart: 7, of which 7 were waited for; matrix products, arithmetic and copies ran while one was open for 1% of the time, Pallas kernels for 0%

commit v1 on v0

--- a/solution.py
+++ b/solution.py
@@ -89,7 +89,15 @@
     width = skip_stream.shape[1]
     slot_cap = 2
     expert_range = lax.broadcasted_iota(jnp.int32, (experts,), 0)
-    all_routes = lax.all_gather(routed_specialist_indices, ("expert", "dp"), axis=0, tiled=True)
+    all_routes = jnp.concatenate(
+        lax.all_to_all(
+            jnp.stack([routed_specialist_indices] * lax.axis_size(("expert", "dp"))),
+            ("expert", "dp"),
+            0,
+            0,
+        ),
+        axis=0,
+    )
     all_hot = jnp.sum(
         (all_routes[:, :, None] == expert_range[None, None, :]).astype(jnp.int32), axis=1
     )

time: 1610 us -> 472 us (0.29)
  blocking collectives: 1320 us -> 56.9 us
  waiting for transfers between devices: 191 us -> 290 us
  starting transfers between devices: 33.8 us -> 58.1 us
    all_gather x1 -> x0, blocking collectives: 1250 us -> none  [per_device(): lax.all_gather(routed_specialist_indices, ('expert', 'dp'), axis=0, tiled...]
    all_to_all x0 -> x1, waiting for transfers between devices: none -> 97.8 us  [per_device(): lax.all_to_all(jnp.stack([routed_specialist_indices] * lax.axis_size(('ex...]
    all_to_all x0 -> x1, starting transfers between devices: none -> 24.3 us  [per_device(): lax.all_to_all(jnp.stack([routed_specialist_indices] * lax.axis_size(('ex...]
  transfers between devices with their start and end apart: 7 -> 8, of which waited for: 7 -> 8; matrix products, arithmetic and copies ran while one was open for 1% -> 3% of each run, Pallas kernels for 0% -> 0%
where the time goes in v1:
time: 472 us; the launch traced here: 471 us
  waiting for transfers between devices  290 us (61%)
  starting transfers between devices  58.1 us (12%)
  blocking collectives  56.9 us (12%)
  local copies, waits for them, and re-layouts  23.7 us (5%)
  between operations  17.5 us (4%)
  other arithmetic  12.9 us (3%)
  matrix products  12.8 us (3%)
    all_to_all x1, waiting for transfers between devices, per_device(): lax.all_to_all(jnp.stack([routed_specialist_indices] * lax.axis_size(('ex...  97.8 us
    all_gather x1, waiting for transfers between devices, per_device(): column_rows = lax.all_gather(arrived_rows, 'dp', axis=1, tiled=True)  92.9 us
    all_to_all x1, blocking collectives, per_device(): lax.all_to_all(outgoing, 'expert', split_axis=0, concat_axis=0, tiled=True)  56.9 us
    all_gather x1, waiting for transfers between devices, per_device(): lax.all_gather(hidden, 'dp', axis=2, tiled=True)  48.3 us
    ppermute x3, waiting for transfers between devices, swapped(): return lax.ppermute(value, axis, pairs)  40.8 us
    all_to_all x1, starting transfers between devices, per_device(): lax.all_to_all(jnp.stack([routed_specialist_indices] * lax.axis_size(('ex...  24.3 us
    all_to_all x1, starting transfers between devices, per_device(): lax.all_to_all(results, 'expert', split_axis=0, concat_axis=0, tiled=True)  18.1 us
    ppermute x3, starting transfers between devices, swapped(): return lax.ppermute(value, axis, pairs)  11.7 us
  transfers between devices with their start and end apart: 8, of which 8 were waited for; matrix products, arithmetic and copies ran while one was open for 3% of the time, Pallas kernels for 0%

profile of v1, /device:TPU:1, one launch (start us, length us, event | category | flops | bytes accessed | tf_op | source)
XLA Modules:
  0.0 471.4 jit_solution(12490455466653314028)
XLA Ops:
  9.5 24.3 %all-to-all-start = ((s32[512,8,8]{1,2,0:T(8,128)}), s32[512,8,8]{1,2,0:T(8,128)S(1)}, u32[]{:S(2)}, u32[]{:S(2)}) async-start(s32[512,8,8]{1,2,0:T(8,128)} %stack.2), calls=%async_computation | async-start | bytes 4194304 | tf_op jit(solution)/shard_map/all_to_all | solution.py:93
  38.6 97.8 %all-to-all-done = s32[512,8,8]{1,2,0:T(8,128)S(1)} async-done(((s32[512,8,8]{1,2,0:T(8,128)}), s32[512,8,8]{1,2,0:T(8,128)S(1)}, u32[]{:S(2)}, u32[]{:S(2)}) %all-to-all-start) | async-done | bytes 131104 | tf_op jit(solution)/shard_map/all_to_all | solution.py:93
  138.1 2.8 eq.58
  140.9 1.9 convert_reduce_fusion
  145.5 56.9 %all_to_all.30 = bf16[64,2,4096]{2,1,0:T(2,128)(2,1)S(1)} all-to-all(bf16[64,2,4096]{2,1,0:T(2,128)(2,1)S(1)} %reshape.131), channel_id=1, replica_groups=mesh['expert'=64,'dp'=8] {'expert'}, dimensions={0} | all-to-all | bytes 2097152 | tf_op jit(solution)/shard_map/all_to_all | solution.py:144
  204.4 92.9 %all-gather.3.cloned.1.call-done = bf16[64,16,4096]{2,0,1:T(8,128)(2,1)} async-done(((bf16[64,2,4096]{2,0,1:T(8,128)(2,1)}), bf16[64,16,4096]{2,0,1:T(8,128)(2,1)}) %all-gather.3.cloned.1.call-update) | async-done | bytes 8388624 | tf_op jit(solution)/shard_map/all_gather | solution.py:145
  297.3 5.9 %fusion.8 = f32[64,16,96]{2,0,1:T(8,128)S(1)} fusion(bf16[64,16,4096]{2,0,1:T(8,128)(2,1)} %all-gather.3.cloned.1.call-done, bf16[1,96,4096]{2,1,0:T(8,128)(2,1)S(1)} %copy-done.2), kind=kOutput, calls=%fused_computation.19 | convolution fusion | flops 805306368 | bytes 9568256 | tf_op jit(solution)/shard_map/esf,hf->esh/dot_general | solution.py:146
  303.2 2.4 fusion
  306.7 48.3 %all-gather.5.cloned.1.call-done = bf16[64,16,768]{0,1,2:T(8,128)(2,1)} async-done(((bf16[64,16,96]{0,1,2:T(8,128)(2,1)}), bf16[64,16,768]{0,1,2:T(8,128)(2,1)}) %all-gather.5.cloned.1.call-update) | async-done | bytes 1572880 | tf_op jit(solution)/shard_map/all_gather | solution.py:156
  355.0 5.5 %copy.72 = bf16[64,16,768]{2,1,0:T(8,128)(2,1)S(1)} copy(bf16[64,16,768]{0,1,2:T(8,128)(2,1)} %all-gather.5.cloned.1.call-done) | data formatting | bytes 3145728 | tf_op jit(solution)/shard_map/all_gather | solution.py:156
  360.5 2.1 convolution_convert_fusion
  363.9 18.1 %all-to-all-start.2 = ((bf16[64,8,2,512]{3,2,1,0:T(2,128)(2,1)}), bf16[64,8,2,512]{3,2,1,0:T(2,128)(2,1)S(1)}, u32[]{:S(2)}, u32[]{:S(2)}) async-start(bf16[64,8,2,512]{3,2,1,0:T(2,128)(2,1)} %reshape.132), calls=%async_computation.2 | async-start | bytes 2097152 | tf_op jit(solution)/shard_map/all_to_all | solution.py:162
  381.9 4.9 %collective-permute-start.2 = (bf16[768,512]{1,0:T(8,128)(2,1)}, bf16[768,512]{1,0:T(8,128)(2,1)}, u32[]{:S(2)}, u32[]{:S(2)}) collective-permute-start(bf16[768,512]{1,0:T(8,128)(2,1)} %bitcast.82), channel_id=1, source_target_pairs={{0,256},{8,264},{16,272},{24,280},{32,288},{40,296},{48,304},{56,3... | collective-permute-start | bytes 2359304 | tf_op jit(solution)/shard_map/ppermute | solution.py:14
  386.8 1.9 collective-permute-start.1
  388.8 4.9 %collective-permute-start = (bf16[96,4096]{1,0:T(8,128)(2,1)}, bf16[96,4096]{1,0:T(8,128)(2,1)S(1)}, u32[]{:S(2)}, u32[]{:S(2)}) collective-permute-start(bf16[96,4096]{1,0:T(8,128)(2,1)} %bitcast.84), channel_id=1, source_target_pairs={{0,256},{8,264},{16,272},{24,280},{32,288},{40,296},{48,304},{56,3... | collective-permute-start | bytes 2359304 | tf_op jit(solution)/shard_map/ppermute | solution.py:14
  397.6 10.7 %collective-permute-done.2 = bf16[768,512]{1,0:T(8,128)(2,1)} collective-permute-done((bf16[768,512]{1,0:T(8,128)(2,1)}, bf16[768,512]{1,0:T(8,128)(2,1)}, u32[]{:S(2)}, u32[]{:S(2)}) %collective-permute-start.2) | collective-permute-done | bytes 786464 | tf_op jit(solution)/shard_map/ppermute | solution.py:14
  408.3 2.1 select_bitcast_fusion
  410.4 20.9 %collective-permute-done.1 = bf16[96,4096]{1,0:T(8,128)(2,1)S(1)} collective-permute-done((bf16[96,4096]{1,0:T(8,128)(2,1)}, bf16[96,4096]{1,0:T(8,128)(2,1)S(1)}, u32[]{:S(2)}, u32[]{:S(2)}) %collective-permute-start.1) | collective-permute-done | bytes 786464 | tf_op jit(solution)/shard_map/ppermute | solution.py:14
  431.3 2.1 select_bitcast_fusion.1
  433.8 1.8 copy.73
  435.6 3.8 all-to-all-start.3
  439.4 9.1 %collective-permute-done = bf16[96,4096]{1,0:T(8,128)(2,1)S(1)} collective-permute-done((bf16[96,4096]{1,0:T(8,128)(2,1)}, bf16[96,4096]{1,0:T(8,128)(2,1)S(1)}, u32[]{:S(2)}, u32[]{:S(2)}) %collective-permute-start) | collective-permute-done | bytes 786464 | tf_op jit(solution)/shard_map/ppermute | solution.py:14
  448.5 2.1 select_bitcast_fusion.2
  450.6 9.3 %all-to-all-done.3 = bf16[64,8,2,512]{3,2,0,1:T(2,128)(2,1)S(1)} async-done(((bf16[64,8,2,512]{3,2,0,1:T(2,128)(2,1)}), bf16[64,8,2,512]{3,2,0,1:T(2,128)(2,1)S(1)}, u32[]{:S(2)}, u32[]{:S(2)}) %all-to-all-start.3) | async-done | bytes 1048608 | tf_op jit(solution)/shard_map/all_to_all | solution.py:161
  (68 shorter events, 21.5 us)
Async XLA Ops:
  7.2 30.6 %copy-start = (bf16[8,16,512]{2,1,0:T(8,128)(2,1)S(1)}, bf16[8,16,512]{2,1,0:T(8,128)(2,1)}, u32[]{:S(2)}) copy-start(bf16[8,16,512]{2,1,0:T(8,128)(2,1)} %param.18) | copy-start | bytes 393220
  7.2 31.2 %copy-start.4 = (s32[8,8]{1,0:T(8,128)S(1)}, s32[8,8]{1,0:T(8,128)}, u32[]{:S(2)}) copy-start(s32[8,8]{1,0:T(8,128)} %param.23) | copy-start | bytes 772
  7.2 30.9 %copy-start.3 = (bf16[8,4096]{1,0:T(8,128)(2,1)S(1)}, bf16[8,4096]{1,0:T(8,128)(2,1)}, u32[]{:S(2)}) copy-start(bf16[8,4096]{1,0:T(8,128)(2,1)} %param.15) | copy-start | bytes 196612
  7.2 31.1 %copy-start.5 = (f32[4096]{0:T(1024)S(1)}, f32[4096]{0:T(1024)}, u32[]{:S(2)}) copy-start(f32[4096]{0:T(1024)} %param.22) | copy-start | bytes 49156
  9.5 133.4 %copy-start.7 = (s32[64]{0:T(128)S(1)}, s32[64]{0:T(128)}, u32[]{:S(2)}) copy-start(s32[64]{0:T(128)} %param.25) | copy-start | bytes 772
  9.5 126.8 %all-to-all-start = ((s32[512,8,8]{1,2,0:T(8,128)}), s32[512,8,8]{1,2,0:T(8,128)S(1)}, u32[]{:S(2)}, u32[]{:S(2)}) async-start(s32[512,8,8]{1,2,0:T(8,128)} %stack.2), calls=%async_computation | async-start | bytes 4194304 | tf_op jit(solution)/shard_map/all_to_all | solution.py:93
  33.8 263.5 %all-gather.3.cloned.1.call-start = ((), (), s32[]{:S(2)}) async-start(), calls=%async_computation.4 | async-start | bytes 9437184 | tf_op jit(solution)/shard_map/all_gather | solution.py:145
  143.6 153.7 %copy-start.2 = (bf16[1,96,4096]{2,1,0:T(8,128)(2,1)S(1)}, bf16[1,96,4096]{2,1,0:T(8,128)(2,1)}, u32[]{:S(2)}) copy-start(bf16[1,96,4096]{2,1,0:T(8,128)(2,1)} %param.27) | copy-start | bytes 2359300
  204.1 99.1 %copy-start.1 = (bf16[1,96,4096]{2,1,0:T(8,128)(2,1)S(1)}, bf16[1,96,4096]{2,1,0:T(8,128)(2,1)}, u32[]{:S(2)}) copy-start(bf16[1,96,4096]{2,1,0:T(8,128)(2,1)} %param.28) | copy-start | bytes 2359300
  204.1 150.9 %all-gather.5.cloned.1.call-start = ((), (), s32[]{:S(2)}) async-start(), calls=%async_computation.5 | async-start | bytes 3538944 | tf_op jit(solution)/shard_map/all_gather | solution.py:156
  297.3 5.9 %copy-start.8 = (bf16[64,16,4096]{2,0,1:T(8,128)(2,1)S(1)}, bf16[64,16,4096]{2,0,1:T(8,128)(2,1)}, u32[]{:S(2)}) copy-start(bf16[64,16,4096]{2,0,1:T(8,128)(2,1)} %all-gather.3.cloned.1.call-done) | copy-start | bytes 25165828
  305.6 88.1 %copy-start.9 = (s32[64]{0:T(128)S(1)}, s32[64]{0:T(128)}, u32[]{:S(2)}) copy-start(s32[64]{0:T(128)} %param.26) | copy-start | bytes 772
  305.6 91.9 %copy-start.6 = (f32[8,8]{1,0:T(8,128)S(1)}, f32[8,8]{1,0:T(8,128)}, u32[]{:S(2)}) copy-start(f32[8,8]{1,0:T(8,128)} %param.24) | copy-start | bytes 772
  363.9 69.9 %all-to-all-start.2 = ((bf16[64,8,2,512]{3,2,1,0:T(2,128)(2,1)}), bf16[64,8,2,512]{3,2,1,0:T(2,128)(2,1)S(1)}, u32[]{:S(2)}, u32[]{:S(2)}) async-start(bf16[64,8,2,512]{3,2,1,0:T(2,128)(2,1)} %reshape.132), calls=%async_computation.2 | async-start | bytes 2097152 | tf_op jit(solution)/shard_map/all_to_all | solution.py:162
  381.9 26.4 %collective-permute-start.2 = (bf16[768,512]{1,0:T(8,128)(2,1)}, bf16[768,512]{1,0:T(8,128)(2,1)}, u32[]{:S(2)}, u32[]{:S(2)}) collective-permute-start(bf16[768,512]{1,0:T(8,128)(2,1)} %bitcast.82), channel_id=1, source_target_pairs={{0,256},{8,264},{16,272},{24,280},{32,288},{40,296},{48,304},{56,3... | collective-permute-start | bytes 2359304 | tf_op jit(solution)/shard_map/ppermute | solution.py:14
  386.8 44.5 %collective-permute-start.1 = (bf16[96,4096]{1,0:T(8,128)(2,1)}, bf16[96,4096]{1,0:T(8,128)(2,1)S(1)}, u32[]{:S(2)}, u32[]{:S(2)}) collective-permute-start(bf16[96,4096]{1,0:T(8,128)(2,1)} %bitcast.83), channel_id=1, source_target_pairs={{0,256},{8,264},{16,272},{24,280},{32,288},{40,296},{48,304},{56,3... | collective-permute-start | bytes 2359304 | tf_op jit(solution)/shard_map/ppermute | solution.py:14
  388.8 59.7 %collective-permute-start = (bf16[96,4096]{1,0:T(8,128)(2,1)}, bf16[96,4096]{1,0:T(8,128)(2,1)S(1)}, u32[]{:S(2)}, u32[]{:S(2)}) collective-permute-start(bf16[96,4096]{1,0:T(8,128)(2,1)} %bitcast.84), channel_id=1, source_target_pairs={{0,256},{8,264},{16,272},{24,280},{32,288},{40,296},{48,304},{56,3... | collective-permute-start | bytes 2359304 | tf_op jit(solution)/shard_map/ppermute | solution.py:14
  435.6 24.3 %all-to-all-start.3 = ((bf16[64,8,2,512]{3,2,0,1:T(2,128)(2,1)}), bf16[64,8,2,512]{3,2,0,1:T(2,128)(2,1)S(1)}, u32[]{:S(2)}, u32[]{:S(2)}) async-start(bf16[64,8,2,512]{3,2,0,1:T(2,128)(2,1)} %copy.73), calls=%async_computation.3 | async-start | bytes 2097152 | tf_op jit(solution)/shard_map/all_to_all | solution.py:161
Sparse Core Ops, SparseCore 0:
  204.3 93.0 all-gather.2
  306.8 48.1 all-gather.4
